TPU v7x, 32 devices: a whole 2x2x4 slice. The times are simulated.
32 devices in a mesh: circ: 4 (over z), normal: 2 (over y), span: 4 (over x, core).
Axes of the slice: x: 2, y: 2, z: 4, core: 2. Of those that a mesh axis runs over, the one named last changes fastest.
Arguments:
- adjoint: float32 [5, 16, 32, 512], P(None, 'span', 'normal', 'circ'), may hold values from -6 to 6
- objective_grad: float32 [5, 16, 32, 512], P(None, 'span', 'normal', 'circ'), may hold values from -6 to 6
- face_weights: float32 [3, 16, 32, 512], P(None, 'span', 'normal', 'circ'), may hold values from 0.2 to 2
- owner_jac: float32 [3, 5, 5], replicated, may hold values from -2.5 to 2.5
- neighbor_jac: float32 [3, 5, 5], replicated, may hold values from -2.5 to 2.5
- coupling: float32 [3, 5], replicated, may hold values from -2.5 to 2.5
- stiffness: float32 [16, 32, 512], P('span', 'normal', 'circ'), may hold values from 0.3 to 3
- wall_kernel: float32 [16, 32, 512], P('span', 'normal', 'circ'), may hold values from -0.25 to 0.25
- panel_owner: int32 [16, 512], P('span', 'circ'), may hold values from 0 to 511, as said below
Outputs:
- adjoint_residual: float32 [5, 16, 32, 512], P(None, 'span', 'normal', 'circ')
- mesh_adjoint: float32 [3, 16, 32, 512], P(None, 'span', 'normal', 'circ')
- panel_sens: float32 [3, 512], P(None, 'span')
Inputs may be any that keep to these rules, and one draw needn't show every extreme that they name: `panel_owner`: the panel of a wall face at station k is owned by span index k // 4 or the one beside it; panels hold ragged numbers of faces.
All inputs are finite; a program needn't handle non-finite values.
Results may differ from a plain program's by a relative error of at most 0.00011.
Values sent between devices are 32-bit elements; how exact they have to be, the bound alone decides.
No kernel may reach another device: no remote copies, remote signals or barrier semaphores. Data moves between devices by JAX's collectives and lax.ppermute only.
A program may use at most 64 MiB of HBM per device.

v0:
```python
import jax
import jax.numpy as jnp
from jax import lax
from jax.sharding import PartitionSpec as P

PANEL_DEV = 128
SWEEPS = 4


def padded_2(array, sides, width, wrap):
    for axis, dim in sides:
        peers, length = (lax.axis_size(axis), array.shape[dim])
        up = [(i, (i + 1) % peers) for i in range(peers if wrap else peers - 1)]
        down = [(j, i) for i, j in up]
        last = lax.slice_in_dim(array, length - width, length, axis=dim)
        initial = lax.slice_in_dim(array, 0, width, axis=dim)
        before = lax.ppermute(last, axis, up)
        after = lax.ppermute(initial, axis, down)
        array = jnp.concatenate([before, array, after], axis=dim)
    return array


def neighbor_sum(padded):
    total = padded[:, 2:, 1:-1, 1:-1] + padded[:, :-2, 1:-1, 1:-1]
    total = total + padded[:, 1:-1, 2:, 1:-1] + padded[:, 1:-1, :-2, 1:-1]
    return total + padded[:, 1:-1, 1:-1, 2:] + padded[:, 1:-1, 1:-1, :-2]


def inner(field):
    return field[:, 1:-1, 1:-1, 1:-1]


def flux_transpose(padded, owner_jac, neighbor_jac):
    psi = padded[:5]
    weights = padded[5:]
    center = inner(psi)
    total = jnp.zeros_like(center)
    for direction in range(3):
        lower = [slice(None), slice(1, -1), slice(1, -1), slice(1, -1)]
        upper = [slice(None), slice(1, -1), slice(1, -1), slice(1, -1)]
        lower[direction + 1] = slice(0, -2)
        upper[direction + 1] = slice(2, None)
        w_here = weights[direction, 1:-1, 1:-1, 1:-1]
        w_lower = weights[direction][tuple(lower[1:])]
        up_term = w_here[None] * (center - psi[tuple(upper)])
        down_term = w_lower[None] * (psi[tuple(lower)] - center)
        total = total + jnp.einsum(
            "uv,ukji->vkji", owner_jac[direction], up_term, precision=lax.Precision.HIGHEST
        )
        total = total + jnp.einsum(
            "uv,ukji->vkji", neighbor_jac[direction], down_term, precision=lax.Precision.HIGHEST
        )
    return total


def relax(mesh_pad, stiff_pad, force_pad):
    weighted = stiff_pad[None] * mesh_pad
    stiff_in = stiff_pad[1:-1, 1:-1, 1:-1]
    diag_term = 6.0 * stiff_in + 1.0
    mesh_in = inner(mesh_pad)
    return (
        mesh_in
        + 0.8
        * (inner(force_pad) - diag_term[None] * mesh_in + neighbor_sum(weighted))
        / diag_term[None]
    )


def run_sweeps(stiff_pad, force_pad):
    mesh_pad = 0.8 * force_pad / (6.0 * stiff_pad[None] + 1.0)
    for sweep in range(1, SWEEPS):
        mesh_pad = relax(mesh_pad, stiff_pad, force_pad)
        stiff_pad = stiff_pad[1:-1, 1:-1, 1:-1]
        force_pad = inner(force_pad)
    return mesh_pad


def on_device(
    adjoint,
    objective_grad,
    face_weights,
    owner_jac,
    neighbor_jac,
    coupling,
    stiffness,
    wall_kernel,
    panel_owner,
):
    stacked = jnp.concatenate([adjoint, face_weights], axis=0)
    beside_all = padded_2(stacked, (("circ", 3),), 1, True)
    padded = padded_2(beside_all, (("normal", 2), ("span", 1)), 1, False)
    residual = flux_transpose(padded, owner_jac, neighbor_jac) + adjoint - objective_grad
    forcing = jnp.einsum("mv,vkji->mkji", coupling, residual, precision=lax.Precision.HIGHEST)
    margin = SWEEPS - 1
    joined = jnp.concatenate([stiffness[None], forcing], axis=0)
    cycle_pad = padded_2(joined, (("circ", 3),), margin, True)
    full_pad = padded_2(cycle_pad, (("normal", 2), ("span", 1)), margin, False)
    mesh = run_sweeps(full_pad[0], full_pad[1:])
    wall_sens = jnp.sum(wall_kernel[None] * mesh, axis=2)
    panel_count = PANEL_DEV * lax.axis_size("span")
    onehot = (
        panel_owner[:, :, None] == jnp.arange(panel_count, dtype=jnp.int32)[None, None, :]
    ).astype(jnp.float32)
    terms = jnp.einsum("mki,kip->mp", wall_sens, onehot, precision=lax.Precision.HIGHEST)
    total = lax.psum(terms, ("circ", "normal", "span"))
    panels = lax.dynamic_slice_in_dim(total, lax.axis_index("span") * PANEL_DEV, PANEL_DEV, 1)
    return (residual, mesh, panels)


def solution(mesh):
    placed = (
        P(None, "span", "normal", "circ"),
        P(None, "span", "normal", "circ"),
        P(None, "span", "normal", "circ"),
        P(),
        P(),
        P(),
        P("span", "normal", "circ"),
        P("span", "normal", "circ"),
        P("span", "circ"),
    )
    return jax.shard_map(
        on_device,
        mesh=mesh,
        in_specs=placed,
        out_specs=(
            P(None, "span", "normal", "circ"),
            P(None, "span", "normal", "circ"),
            P(None, "span"),
        ),
        check_vma=False,
    )
```

profile of v0, /device:TPU:14, one launch (start us, length us, event | category | flops | bytes accessed | tf_op | source)
XLA Modules:
  0.0 115.0 jit_solution(1528439476088058492)
XLA Ops:
  0.7 1.0 constant_dynamic-update-slice_fusion.1
  1.8 1.6 %collective-permute-start = (f32[8,4,16,1]{3,2,1,0:T(8,128)S(1)}, f32[8,4,16,1]{3,2,1,0:T(8,128)S(1)}, u32[]{:S(2)}, u32[]{:S(2)}) collective-permute-start(f32[8,4,16,1]{3,2,1,0:T(8,128)S(1)} %get-tuple-element.32), channel_id=1, source_target_pairs={{0,8},{8,16},{16,24},{24,0},{1,9},{9,17},{17,25},{25,1},{2,10},{10... | collective-permute-start | bytes 6152 | tf_op jit(solution)/shard_map/ppermute | solution.py:17
  3.9 7.2 %collective-permute-done = f32[8,4,16,1]{3,2,1,0:T(8,128)S(1)} collective-permute-done((f32[8,4,16,1]{3,2,1,0:T(8,128)S(1)}, f32[8,4,16,1]{3,2,1,0:T(8,128)S(1)}, u32[]{:S(2)}, u32[]{:S(2)}) %collective-permute-start) | collective-permute-done | bytes 2080 | tf_op jit(solution)/shard_map/ppermute | solution.py:17
  11.0 5.3 %collective-permute-done.1 = f32[8,4,16,1]{3,2,1,0:T(8,128)S(1)} collective-permute-done((f32[8,4,16,1]{3,2,1,0:T(8,128)S(1)}, f32[8,4,16,1]{3,2,1,0:T(8,128)S(1)}, u32[]{:S(2)}, u32[]{:S(2)}) %collective-permute-start.1) | collective-permute-done | bytes 2080 | tf_op jit(solution)/shard_map/ppermute | solution.py:18
  16.6 1.3 %collective-permute-start.2 = (f32[8,4,1,130]{3,2,1,0:T(1,128)S(1)}, f32[8,4,1,130]{3,2,1,0:T(1,128)S(1)}, u32[]{:S(2)}, u32[]{:S(2)}) collective-permute-start(f32[8,4,1,130]{3,2,1,0:T(1,128)S(1)} %get-tuple-element.24), channel_id=1, source_target_pairs={{0,4},{1,5},{2,6},{3,7},{8,12},{9,13},{10,14},{11,15},{16,20},{17,... | collective-permute-start | bytes 49928 | tf_op jit(solution)/shard_map/ppermute | solution.py:17
  17.9 4.5 %collective-permute-start.3 = (f32[8,4,1,130]{3,2,1,0:T(1,128)S(1)}, f32[8,4,1,130]{3,2,1,0:T(1,128)S(1)}, u32[]{:S(2)}, u32[]{:S(2)}) collective-permute-start(f32[8,4,1,130]{3,2,1,0:T(1,128)S(1)} %get-tuple-element.25), channel_id=1, source_target_pairs={{4,0},{5,1},{6,2},{7,3},{12,8},{13,9},{14,10},{15,11},{20,16},{21,... | collective-permute-start | bytes 49928 | tf_op jit(solution)/shard_map/ppermute | solution.py:18
  22.5 1.5 %collective-permute-done.3 = f32[8,4,1,130]{3,2,1,0:T(1,128)S(1)} collective-permute-done((f32[8,4,1,130]{3,2,1,0:T(1,128)S(1)}, f32[8,4,1,130]{3,2,1,0:T(1,128)S(1)}, u32[]{:S(2)}, u32[]{:S(2)}) %collective-permute-start.3) | collective-permute-done | bytes 16672 | tf_op jit(solution)/shard_map/ppermute | solution.py:18
  24.3 1.9 %collective-permute-start.5 = (f32[8,1,18,130]{3,2,1,0:T(8,128)S(1)}, f32[8,1,18,130]{3,2,1,0:T(8,128)S(1)}, u32[]{:S(2)}, u32[]{:S(2)}) collective-permute-start(f32[8,1,18,130]{3,2,1,0:T(8,128)S(1)} %get-tuple-element.22), channel_id=1, source_target_pairs={{0,1},{1,2},{2,3},{4,5},{5,6},{6,7},{8,9},{9,10},{10,11},{12,13},{... | collective-permute-start | bytes 224648 | tf_op jit(solution)/shard_map/ppermute | solution.py:17
  26.2 3.6 %collective-permute-start.4 = (f32[8,1,18,130]{3,2,1,0:T(8,128)S(1)}, f32[8,1,18,130]{3,2,1,0:T(8,128)S(1)}, u32[]{:S(2)}, u32[]{:S(2)}) collective-permute-start(f32[8,1,18,130]{3,2,1,0:T(8,128)S(1)} %get-tuple-element.23), channel_id=1, source_target_pairs={{1,0},{2,1},{3,2},{5,4},{6,5},{7,6},{9,8},{10,9},{11,10},{13,12},{... | collective-permute-start | bytes 224648 | tf_op jit(solution)/shard_map/ppermute | solution.py:18
  29.9 1.4 %collective-permute-done.5 = f32[8,1,18,130]{3,2,1,0:T(8,128)S(1)} collective-permute-done((f32[8,1,18,130]{3,2,1,0:T(8,128)S(1)}, f32[8,1,18,130]{3,2,1,0:T(8,128)S(1)}, u32[]{:S(2)}, u32[]{:S(2)}) %collective-permute-start.5) | collective-permute-done | bytes 74912 | tf_op jit(solution)/shard_map/ppermute | solution.py:17
  31.3 1.8 %collective-permute-done.4 = f32[8,1,18,130]{3,2,1,0:T(8,128)S(1)} collective-permute-done((f32[8,1,18,130]{3,2,1,0:T(8,128)S(1)}, f32[8,1,18,130]{3,2,1,0:T(8,128)S(1)}, u32[]{:S(2)}, u32[]{:S(2)}) %collective-permute-start.4) | collective-permute-done | bytes 74912 | tf_op jit(solution)/shard_map/ppermute | solution.py:18
  33.5 0.7 copy-done.1
  37.4 0.6 fusion.2
  39.0 0.8 collective-permute-start.6
  39.8 1.3 %collective-permute-start.7 = (f32[4,4,16,3]{3,0,2,1:T(4,128)S(1)}, f32[4,4,16,3]{3,0,2,1:T(4,128)S(1)}, u32[]{:S(2)}, u32[]{:S(2)}) collective-permute-start(f32[4,4,16,3]{3,0,2,1:T(4,128)S(1)} %get-tuple-element.39), channel_id=1, source_target_pairs={{8,0},{16,8},{24,16},{0,24},{9,1},{17,9},{25,17},{1,25},{10,2},{18... | collective-permute-start | bytes 9224 | tf_op jit(solution)/shard_map/ppermute | solution.py:18
  41.1 2.9 %collective-permute-done.6 = f32[4,4,16,3]{3,0,2,1:T(4,128)S(1)} collective-permute-done((f32[4,4,16,3]{3,0,2,1:T(4,128)S(1)}, f32[4,4,16,3]{3,0,2,1:T(4,128)S(1)}, u32[]{:S(2)}, u32[]{:S(2)}) %collective-permute-start.6) | collective-permute-done | bytes 3104 | tf_op jit(solution)/shard_map/ppermute | solution.py:17
  44.0 2.1 %collective-permute-done.7 = f32[4,4,16,3]{3,0,2,1:T(4,128)S(1)} collective-permute-done((f32[4,4,16,3]{3,0,2,1:T(4,128)S(1)}, f32[4,4,16,3]{3,0,2,1:T(4,128)S(1)}, u32[]{:S(2)}, u32[]{:S(2)}) %collective-permute-start.7) | collective-permute-done | bytes 3104 | tf_op jit(solution)/shard_map/ppermute | solution.py:18
  46.4 1.3 %collective-permute-start.8 = (f32[4,4,3,134]{3,0,2,1:T(4,128)S(1)}, f32[4,4,3,134]{3,0,2,1:T(4,128)S(1)}, u32[]{:S(2)}, u32[]{:S(2)}) collective-permute-start(f32[4,4,3,134]{3,0,2,1:T(4,128)S(1)} %get-tuple-element.28), channel_id=1, source_target_pairs={{0,4},{1,5},{2,6},{3,7},{8,12},{9,13},{10,14},{11,15},{16,20},{17,... | collective-permute-start | bytes 77192 | tf_op jit(solution)/shard_map/ppermute | solution.py:17
  47.7 4.5 %collective-permute-start.9 = (f32[4,4,3,134]{3,0,2,1:T(4,128)S(1)}, f32[4,4,3,134]{3,0,2,1:T(4,128)S(1)}, u32[]{:S(2)}, u32[]{:S(2)}) collective-permute-start(f32[4,4,3,134]{3,0,2,1:T(4,128)S(1)} %get-tuple-element.29), channel_id=1, source_target_pairs={{4,0},{5,1},{6,2},{7,3},{12,8},{13,9},{14,10},{15,11},{20,16},{21,... | collective-permute-start | bytes 77192 | tf_op jit(solution)/shard_map/ppermute | solution.py:18
  52.4 1.6 %collective-permute-done.9 = f32[4,4,3,134]{3,0,2,1:T(4,128)S(1)} collective-permute-done((f32[4,4,3,134]{3,0,2,1:T(4,128)S(1)}, f32[4,4,3,134]{3,0,2,1:T(4,128)S(1)}, u32[]{:S(2)}, u32[]{:S(2)}) %collective-permute-start.9) | collective-permute-done | bytes 25760 | tf_op jit(solution)/shard_map/ppermute | solution.py:18
  54.4 1.9 %collective-permute-start.10 = (f32[4,3,22,134]{3,0,2,1:T(4,128)S(1)}, f32[4,3,22,134]{3,0,2,1:T(4,128)S(1)}, u32[]{:S(2)}, u32[]{:S(2)}) collective-permute-start(f32[4,3,22,134]{3,0,2,1:T(4,128)S(1)} %get-tuple-element.30), channel_id=1, source_target_pairs={{0,1},{1,2},{2,3},{4,5},{5,6},{6,7},{8,9},{9,10},{10,11},{12,13},{... | collective-permute-start | bytes 424520 | tf_op jit(solution)/shard_map/ppermute | solution.py:17
  56.4 3.8 %collective-permute-start.11 = (f32[4,3,22,134]{3,0,2,1:T(4,128)S(1)}, f32[4,3,22,134]{3,0,2,1:T(4,128)S(1)}, u32[]{:S(2)}, u32[]{:S(2)}) collective-permute-start(f32[4,3,22,134]{3,0,2,1:T(4,128)S(1)} %get-tuple-element.31), channel_id=1, source_target_pairs={{1,0},{2,1},{3,2},{5,4},{6,5},{7,6},{9,8},{10,9},{11,10},{13,12},{... | collective-permute-start | bytes 424520 | tf_op jit(solution)/shard_map/ppermute | solution.py:18
  60.2 0.7 copy.32
  60.9 1.3 %collective-permute-done.10 = f32[4,3,22,134]{3,0,2,1:T(4,128)S(1)} collective-permute-done((f32[4,3,22,134]{3,0,2,1:T(4,128)S(1)}, f32[4,3,22,134]{3,0,2,1:T(4,128)S(1)}, u32[]{:S(2)}, u32[]{:S(2)}) %collective-permute-start.10) | collective-permute-done | bytes 141536 | tf_op jit(solution)/shard_map/ppermute | solution.py:17
  62.2 1.8 %collective-permute-done.11 = f32[4,3,22,134]{3,0,2,1:T(4,128)S(1)} collective-permute-done((f32[4,3,22,134]{3,0,2,1:T(4,128)S(1)}, f32[4,3,22,134]{3,0,2,1:T(4,128)S(1)}, u32[]{:S(2)}, u32[]{:S(2)}) %collective-permute-start.11) | collective-permute-done | bytes 141536 | tf_op jit(solution)/shard_map/ppermute | solution.py:18
  65.2 0.5 broadcast_multiply_fusion
  65.7 2.4 %broadcast_multiply_fusion.1 = (f32[3,8,20,132]{3,0,2,1:T(4,128)S(1)}, f32[3,8,20,132]{3,0,2,1:T(4,128)S(1)}) fusion(f32[8,20,132]{2,1,0:T(8,128)S(1)} %get-tuple-element.37, f32[3,10,22,134]{3,0,2,1:T(4,128)S(1)} %get-tuple-element.12, f32[8,20,132]{2,1,0:T(8,128)S(1)} %get-tuple-element.36, f32[4,10,22,134]{3,0,2,1:T(4,128)S(1)} %pad_maximum_fusion, ...), kind=kLoop, calls=%fused_computation.35 | loop fusion | flops 760320 | bytes 2703360 | tf_op jit(solution)/shard_map/mul | solution.py:57
  68.2 1.7 %broadcast_multiply_fusion.2 = (f32[3,6,18,130]{3,0,2,1:T(4,128)S(1)}, f32[3,6,18,130]{3,0,2,1:T(4,128)S(1)}) fusion(f32[6,18,130]{2,1,0:T(8,128)S(1)} %get-tuple-element.35, f32[3,8,20,132]{3,0,2,1:T(4,128)S(1)} %get-tuple-element.10, f32[6,18,130]{2,1,0:T(8,128)S(1)} %get-tuple-element.34, f32[4,10,22,134]{3,0,2,1:T(4,128)S(1)} %pad_maximum_fusion, ...), kind=kLoop, calls=%fused_computation.46 | loop fusion | flops 505440 | bytes 1797120 | tf_op jit(solution)/shard_map/mul | solution.py:57
  69.9 0.5 multiply_reduce_fusion
  71.0 42.7 %psum.7 = f32[3,512]{1,0:T(4,128)S(1)} all-reduce(f32[3,512]{1,0:T(4,128)S(1)} %convolution_bitcast_fusion.1), channel_id=1, replica_groups=mesh['circ'=4,'normal'=2,'span'=4] {'circ','normal','span'}, use_global_device_ids=true, to_apply=%region_1.0 | all-reduce | flops 1536 | bytes 12288 | tf_op jit(solution)/shard_map/psum | solution.py:105
  113.7 0.6 copy.33
  114.4 0.6 constant_dynamic-slice_fusion
  (51 shorter events, 8.3 us)
Async XLA Ops:
  0.6 37.4 %copy-start = (f32[3,5]{1,0:T(4,128)S(1)}, f32[3,5]{1,0:T(4,128)}, u32[]{:S(2)}) copy-start(f32[3,5]{1,0:T(4,128)} %param.14) | copy-start | bytes 184
  0.6 1.0 copy-start.4
  1.8 9.2 %collective-permute-start = (f32[8,4,16,1]{3,2,1,0:T(8,128)S(1)}, f32[8,4,16,1]{3,2,1,0:T(8,128)S(1)}, u32[]{:S(2)}, u32[]{:S(2)}) collective-permute-start(f32[8,4,16,1]{3,2,1,0:T(8,128)S(1)} %get-tuple-element.32), channel_id=1, source_target_pairs={{0,8},{8,16},{16,24},{24,0},{1,9},{9,17},{17,25},{25,1},{2,10},{10... | collective-permute-start | bytes 6152 | tf_op jit(solution)/shard_map/ppermute | solution.py:17
  3.4 12.9 %collective-permute-start.1 = (f32[8,4,16,1]{3,2,1,0:T(8,128)S(1)}, f32[8,4,16,1]{3,2,1,0:T(8,128)S(1)}, u32[]{:S(2)}, u32[]{:S(2)}) collective-permute-start(f32[8,4,16,1]{3,2,1,0:T(8,128)S(1)} %get-tuple-element.33), channel_id=1, source_target_pairs={{8,0},{16,8},{24,16},{0,24},{9,1},{17,9},{25,17},{1,25},{10,2},{18... | collective-permute-start | bytes 6152 | tf_op jit(solution)/shard_map/ppermute | solution.py:18
  3.9 18.6 %copy-start.6 = (f32[3,5,5]{2,0,1:T(4,128)S(1)}, f32[3,5,5]{2,0,1:T(4,128)}, u32[]{:S(2)}) copy-start(f32[3,5,5]{2,0,1:T(4,128)} %param.12) | copy-start | bytes 904
  16.6 5.9 %collective-permute-start.2 = (f32[8,4,1,130]{3,2,1,0:T(1,128)S(1)}, f32[8,4,1,130]{3,2,1,0:T(1,128)S(1)}, u32[]{:S(2)}, u32[]{:S(2)}) collective-permute-start(f32[8,4,1,130]{3,2,1,0:T(1,128)S(1)} %get-tuple-element.24), channel_id=1, source_target_pairs={{0,4},{1,5},{2,6},{3,7},{8,12},{9,13},{10,14},{11,15},{16,20},{17,... | collective-permute-start | bytes 49928 | tf_op jit(solution)/shard_map/ppermute | solution.py:17
  17.9 6.1 %collective-permute-start.3 = (f32[8,4,1,130]{3,2,1,0:T(1,128)S(1)}, f32[8,4,1,130]{3,2,1,0:T(1,128)S(1)}, u32[]{:S(2)}, u32[]{:S(2)}) collective-permute-start(f32[8,4,1,130]{3,2,1,0:T(1,128)S(1)} %get-tuple-element.25), channel_id=1, source_target_pairs={{4,0},{5,1},{6,2},{7,3},{12,8},{13,9},{14,10},{15,11},{20,16},{21,... | collective-permute-start | bytes 49928 | tf_op jit(solution)/shard_map/ppermute | solution.py:18
  22.5 7.4 %copy-start.7 = (f32[3,5,5]{2,0,1:T(4,128)S(1)}, f32[3,5,5]{2,0,1:T(4,128)}, u32[]{:S(2)}) copy-start(f32[3,5,5]{2,0,1:T(4,128)} %param.13) | copy-start | bytes 904
  24.3 7.0 %collective-permute-start.5 = (f32[8,1,18,130]{3,2,1,0:T(8,128)S(1)}, f32[8,1,18,130]{3,2,1,0:T(8,128)S(1)}, u32[]{:S(2)}, u32[]{:S(2)}) collective-permute-start(f32[8,1,18,130]{3,2,1,0:T(8,128)S(1)} %get-tuple-element.22), channel_id=1, source_target_pairs={{0,1},{1,2},{2,3},{4,5},{5,6},{6,7},{8,9},{9,10},{10,11},{12,13},{... | collective-permute-start | bytes 224648 | tf_op jit(solution)/shard_map/ppermute | solution.py:17
  26.2 6.8 %collective-permute-start.4 = (f32[8,1,18,130]{3,2,1,0:T(8,128)S(1)}, f32[8,1,18,130]{3,2,1,0:T(8,128)S(1)}, u32[]{:S(2)}, u32[]{:S(2)}) collective-permute-start(f32[8,1,18,130]{3,2,1,0:T(8,128)S(1)} %get-tuple-element.23), channel_id=1, source_target_pairs={{1,0},{2,1},{3,2},{5,4},{6,5},{7,6},{9,8},{10,9},{11,10},{13,12},{... | collective-permute-start | bytes 224648 | tf_op jit(solution)/shard_map/ppermute | solution.py:18
  33.2 0.9 copy-start.1
  36.5 0.9 copy-start.3
  38.0 0.8 copy-start.2
  39.0 5.0 %collective-permute-start.6 = (f32[4,4,16,3]{3,0,2,1:T(4,128)S(1)}, f32[4,4,16,3]{3,0,2,1:T(4,128)S(1)}, u32[]{:S(2)}, u32[]{:S(2)}) collective-permute-start(f32[4,4,16,3]{3,0,2,1:T(4,128)S(1)} %get-tuple-element.38), channel_id=1, source_target_pairs={{0,8},{8,16},{16,24},{24,0},{1,9},{9,17},{17,25},{25,1},{2,10},{10... | collective-permute-start | bytes 9224 | tf_op jit(solution)/shard_map/ppermute | solution.py:17
  39.8 6.4 %collective-permute-start.7 = (f32[4,4,16,3]{3,0,2,1:T(4,128)S(1)}, f32[4,4,16,3]{3,0,2,1:T(4,128)S(1)}, u32[]{:S(2)}, u32[]{:S(2)}) collective-permute-start(f32[4,4,16,3]{3,0,2,1:T(4,128)S(1)} %get-tuple-element.39), channel_id=1, source_target_pairs={{8,0},{16,8},{24,16},{0,24},{9,1},{17,9},{25,17},{1,25},{10,2},{18... | collective-permute-start | bytes 9224 | tf_op jit(solution)/shard_map/ppermute | solution.py:18
  46.4 6.0 %collective-permute-start.8 = (f32[4,4,3,134]{3,0,2,1:T(4,128)S(1)}, f32[4,4,3,134]{3,0,2,1:T(4,128)S(1)}, u32[]{:S(2)}, u32[]{:S(2)}) collective-permute-start(f32[4,4,3,134]{3,0,2,1:T(4,128)S(1)} %get-tuple-element.28), channel_id=1, source_target_pairs={{0,4},{1,5},{2,6},{3,7},{8,12},{9,13},{10,14},{11,15},{16,20},{17,... | collective-permute-start | bytes 77192 | tf_op jit(solution)/shard_map/ppermute | solution.py:17
  47.7 6.3 %collective-permute-start.9 = (f32[4,4,3,134]{3,0,2,1:T(4,128)S(1)}, f32[4,4,3,134]{3,0,2,1:T(4,128)S(1)}, u32[]{:S(2)}, u32[]{:S(2)}) collective-permute-start(f32[4,4,3,134]{3,0,2,1:T(4,128)S(1)} %get-tuple-element.29), channel_id=1, source_target_pairs={{4,0},{5,1},{6,2},{7,3},{12,8},{13,9},{14,10},{15,11},{20,16},{21,... | collective-permute-start | bytes 77192 | tf_op jit(solution)/shard_map/ppermute | solution.py:18
  54.4 7.8 %collective-permute-start.10 = (f32[4,3,22,134]{3,0,2,1:T(4,128)S(1)}, f32[4,3,22,134]{3,0,2,1:T(4,128)S(1)}, u32[]{:S(2)}, u32[]{:S(2)}) collective-permute-start(f32[4,3,22,134]{3,0,2,1:T(4,128)S(1)} %get-tuple-element.30), channel_id=1, source_target_pairs={{0,1},{1,2},{2,3},{4,5},{5,6},{6,7},{8,9},{9,10},{10,11},{12,13},{... | collective-permute-start | bytes 424520 | tf_op jit(solution)/shard_map/ppermute | solution.py:17
  56.4 7.6 %collective-permute-start.11 = (f32[4,3,22,134]{3,0,2,1:T(4,128)S(1)}, f32[4,3,22,134]{3,0,2,1:T(4,128)S(1)}, u32[]{:S(2)}, u32[]{:S(2)}) collective-permute-start(f32[4,3,22,134]{3,0,2,1:T(4,128)S(1)} %get-tuple-element.31), channel_id=1, source_target_pairs={{1,0},{2,1},{3,2},{5,4},{6,5},{7,6},{9,8},{10,9},{11,10},{13,12},{... | collective-permute-start | bytes 424520 | tf_op jit(solution)/shard_map/ppermute | solution.py:18
  68.2 1.7 %copy-start.5 = (f32[4,16,128]{2,1,0:T(8,128)S(1)}, f32[4,16,128]{2,1,0:T(8,128)}, u32[]{:S(2)}) copy-start(f32[4,16,128]{2,1,0:T(8,128)} %param.16) | copy-start | bytes 98308
  69.8 0.7 copy-start.8
where the time goes:
time: 115 us
  blocking collectives  42.7 us (37%)
  starting transfers between devices  27.1 us (24%)
  waiting for transfers between devices  27 us (23%)
  other arithmetic  8.29 us (7%)
  local copies, waits for them, and re-layouts  5.05 us (4%)
  matrix products  3.69 us (3%)
    psum x1, blocking collectives, on_device(): total = lax.psum(terms, ('circ', 'normal', 'span'))  42.7 us
    ppermute x6, starting transfers between devices, padded_2(): after = lax.ppermute(initial, axis, down)  18.3 us
    ppermute x6, waiting for transfers between devices, padded_2(): after = lax.ppermute(initial, axis, down)  14.1 us
    ppermute x6, waiting for transfers between devices, padded_2(): before = lax.ppermute(last, axis, up)  12.9 us
    ppermute x6, starting transfers between devices, padded_2(): before = lax.ppermute(last, axis, up)  8.85 us
    mul x3, other arithmetic, relax(): weighted = stiff_pad[None] * mesh_pad  4.64 us
    unnamed x22, local copies, waits for them, and re-layouts  4.09 us
  transfers between devices with their start and end apart: 12, of which 11 were waited for; matrix products, arithmetic and copies ran while one was open for 1% of the time, Pallas kernels for 0%

commit v1 on v0

--- a/solution.py
+++ b/solution.py
@@ -102,7 +102,7 @@
         panel_owner[:, :, None] == jnp.arange(panel_count, dtype=jnp.int32)[None, None, :]
     ).astype(jnp.float32)
     terms = jnp.einsum("mki,kip->mp", wall_sens, onehot, precision=lax.Precision.HIGHEST)
-    total = lax.psum(terms, ("circ", "normal", "span"))
+    total = jnp.sum(lax.all_gather(terms, ("circ", "normal", "span")), axis=0)
     panels = lax.dynamic_slice_in_dim(total, lax.axis_index("span") * PANEL_DEV, PANEL_DEV, 1)
     return (residual, mesh, panels)
 

time: 115 us -> 117 us (1.017)
  the two profiles are of different devices: /device:TPU:14 before, /device:TPU:0 now
where the time goes in v1:
time: 117 us; the launch traced here: 116 us
  blocking collectives  43.2 us (37%)
  waiting for transfers between devices  31.3 us (27%)
  starting transfers between devices  23.9 us (20%)
  other arithmetic  8.35 us (7%)
  local copies, waits for them, and re-layouts  4.9 us (4%)
  matrix products  3.7 us (3%)
    all_gather x1, blocking collectives, on_device(): total = jnp.sum(lax.all_gather(terms, ('circ', 'normal', 'span')), axis=0)  43.2 us
    ppermute x6, waiting for transfers between devices, padded_2(): after = lax.ppermute(initial, axis, down)  20.4 us
    ppermute x6, starting transfers between devices, padded_2(): before = lax.ppermute(last, axis, up)  13.8 us
    ppermute x6, waiting for transfers between devices, padded_2(): before = lax.ppermute(last, axis, up)  10.9 us
    ppermute x6, starting transfers between devices, padded_2(): after = lax.ppermute(initial, axis, down)  10.1 us
    mul x3, other arithmetic, relax(): weighted = stiff_pad[None] * mesh_pad  4.64 us
    unnamed x22, local copies, waits for them, and re-layouts  3.93 us
  transfers between devices with their start and end apart: 12, of which 10 were waited for; matrix products, arithmetic and copies ran while one was open for 1% of the time, Pallas kernels for 0%

profile of v1, /device:TPU:0, one launch (start us, length us, event | category | flops | bytes accessed | tf_op | source)
XLA Modules:
  0.0 116.4 jit_solution(13396929754676314011)
XLA Ops:
  0.7 1.0 constant_dynamic-update-slice_fusion.1
  1.8 3.1 %collective-permute-start = (f32[8,4,16,1]{3,2,1,0:T(8,128)S(1)}, f32[8,4,16,1]{3,2,1,0:T(8,128)S(1)}, u32[]{:S(2)}, u32[]{:S(2)}) collective-permute-start(f32[8,4,16,1]{3,2,1,0:T(8,128)S(1)} %get-tuple-element.35), channel_id=1, source_target_pairs={{0,8},{8,16},{16,24},{24,0},{1,9},{9,17},{17,25},{25,1},{2,10},{10... | collective-permute-start | bytes 6152 | tf_op jit(solution)/shard_map/ppermute | solution.py:17
  4.9 2.1 %collective-permute-start.1 = (f32[8,4,16,1]{3,2,1,0:T(8,128)S(1)}, f32[8,4,16,1]{3,2,1,0:T(8,128)S(1)}, u32[]{:S(2)}, u32[]{:S(2)}) collective-permute-start(f32[8,4,16,1]{3,2,1,0:T(8,128)S(1)} %get-tuple-element.36), channel_id=1, source_target_pairs={{8,0},{16,8},{24,16},{0,24},{9,1},{17,9},{25,17},{1,25},{10,2},{18... | collective-permute-start | bytes 6152 | tf_op jit(solution)/shard_map/ppermute | solution.py:18
  7.0 7.1 %collective-permute-done = f32[8,4,16,1]{3,2,1,0:T(8,128)S(1)} collective-permute-done((f32[8,4,16,1]{3,2,1,0:T(8,128)S(1)}, f32[8,4,16,1]{3,2,1,0:T(8,128)S(1)}, u32[]{:S(2)}, u32[]{:S(2)}) %collective-permute-start) | collective-permute-done | bytes 2080 | tf_op jit(solution)/shard_map/ppermute | solution.py:17
  14.1 4.2 %collective-permute-done.1 = f32[8,4,16,1]{3,2,1,0:T(8,128)S(1)} collective-permute-done((f32[8,4,16,1]{3,2,1,0:T(8,128)S(1)}, f32[8,4,16,1]{3,2,1,0:T(8,128)S(1)}, u32[]{:S(2)}, u32[]{:S(2)}) %collective-permute-start.1) | collective-permute-done | bytes 2080 | tf_op jit(solution)/shard_map/ppermute | solution.py:18
  18.5 3.4 %collective-permute-start.2 = (f32[8,4,1,130]{3,2,1,0:T(1,128)S(1)}, f32[8,4,1,130]{3,2,1,0:T(1,128)S(1)}, u32[]{:S(2)}, u32[]{:S(2)}) collective-permute-start(f32[8,4,1,130]{3,2,1,0:T(1,128)S(1)} %get-tuple-element.27), channel_id=1, source_target_pairs={{0,4},{1,5},{2,6},{3,7},{8,12},{9,13},{10,14},{11,15},{16,20},{17,... | collective-permute-start | bytes 49928 | tf_op jit(solution)/shard_map/ppermute | solution.py:17
  22.0 1.3 %collective-permute-start.3 = (f32[8,4,1,130]{3,2,1,0:T(1,128)S(1)}, f32[8,4,1,130]{3,2,1,0:T(1,128)S(1)}, u32[]{:S(2)}, u32[]{:S(2)}) collective-permute-start(f32[8,4,1,130]{3,2,1,0:T(1,128)S(1)} %get-tuple-element.28), channel_id=1, source_target_pairs={{4,0},{5,1},{6,2},{7,3},{12,8},{13,9},{14,10},{15,11},{20,16},{21,... | collective-permute-start | bytes 49928 | tf_op jit(solution)/shard_map/ppermute | solution.py:18
  23.5 4.2 %collective-permute-done.3 = f32[8,4,1,130]{3,2,1,0:T(1,128)S(1)} collective-permute-done((f32[8,4,1,130]{3,2,1,0:T(1,128)S(1)}, f32[8,4,1,130]{3,2,1,0:T(1,128)S(1)}, u32[]{:S(2)}, u32[]{:S(2)}) %collective-permute-start.3) | collective-permute-done | bytes 16672 | tf_op jit(solution)/shard_map/ppermute | solution.py:18
  28.0 1.3 %collective-permute-start.5 = (f32[8,1,18,130]{3,2,1,0:T(8,128)S(1)}, f32[8,1,18,130]{3,2,1,0:T(8,128)S(1)}, u32[]{:S(2)}, u32[]{:S(2)}) collective-permute-start(f32[8,1,18,130]{3,2,1,0:T(8,128)S(1)} %get-tuple-element.25), channel_id=1, source_target_pairs={{0,1},{1,2},{2,3},{4,5},{5,6},{6,7},{8,9},{9,10},{10,11},{12,13},{... | collective-permute-start | bytes 224648 | tf_op jit(solution)/shard_map/ppermute | solution.py:17
  29.3 1.3 %collective-permute-start.4 = (f32[8,1,18,130]{3,2,1,0:T(8,128)S(1)}, f32[8,1,18,130]{3,2,1,0:T(8,128)S(1)}, u32[]{:S(2)}, u32[]{:S(2)}) collective-permute-start(f32[8,1,18,130]{3,2,1,0:T(8,128)S(1)} %get-tuple-element.26), channel_id=1, source_target_pairs={{1,0},{2,1},{3,2},{5,4},{6,5},{7,6},{9,8},{10,9},{11,10},{13,12},{... | collective-permute-start | bytes 224648 | tf_op jit(solution)/shard_map/ppermute | solution.py:18
  30.6 3.7 %collective-permute-done.4 = f32[8,1,18,130]{3,2,1,0:T(8,128)S(1)} collective-permute-done((f32[8,1,18,130]{3,2,1,0:T(8,128)S(1)}, f32[8,1,18,130]{3,2,1,0:T(8,128)S(1)}, u32[]{:S(2)}, u32[]{:S(2)}) %collective-permute-start.4) | collective-permute-done | bytes 74912 | tf_op jit(solution)/shard_map/ppermute | solution.py:18
  34.8 0.7 copy-done.1
  38.7 0.6 fusion.2
  40.3 1.2 %collective-permute-start.6 = (f32[4,4,16,3]{3,0,2,1:T(4,128)S(1)}, f32[4,4,16,3]{3,0,2,1:T(4,128)S(1)}, u32[]{:S(2)}, u32[]{:S(2)}) collective-permute-start(f32[4,4,16,3]{3,0,2,1:T(4,128)S(1)} %get-tuple-element.41), channel_id=1, source_target_pairs={{0,8},{8,16},{16,24},{24,0},{1,9},{9,17},{17,25},{25,1},{2,10},{10... | collective-permute-start | bytes 9224 | tf_op jit(solution)/shard_map/ppermute | solution.py:17
  41.5 2.7 %collective-permute-start.7 = (f32[4,4,16,3]{3,0,2,1:T(4,128)S(1)}, f32[4,4,16,3]{3,0,2,1:T(4,128)S(1)}, u32[]{:S(2)}, u32[]{:S(2)}) collective-permute-start(f32[4,4,16,3]{3,0,2,1:T(4,128)S(1)} %get-tuple-element.42), channel_id=1, source_target_pairs={{8,0},{16,8},{24,16},{0,24},{9,1},{17,9},{25,17},{1,25},{10,2},{18... | collective-permute-start | bytes 9224 | tf_op jit(solution)/shard_map/ppermute | solution.py:18
  44.2 3.1 %collective-permute-done.6 = f32[4,4,16,3]{3,0,2,1:T(4,128)S(1)} collective-permute-done((f32[4,4,16,3]{3,0,2,1:T(4,128)S(1)}, f32[4,4,16,3]{3,0,2,1:T(4,128)S(1)}, u32[]{:S(2)}, u32[]{:S(2)}) %collective-permute-start.6) | collective-permute-done | bytes 3104 | tf_op jit(solution)/shard_map/ppermute | solution.py:17
  47.3 0.6 collective-permute-done.7
  48.1 1.6 %collective-permute-start.8 = (f32[4,4,3,134]{3,0,2,1:T(4,128)S(1)}, f32[4,4,3,134]{3,0,2,1:T(4,128)S(1)}, u32[]{:S(2)}, u32[]{:S(2)}) collective-permute-start(f32[4,4,3,134]{3,0,2,1:T(4,128)S(1)} %get-tuple-element.31), channel_id=1, source_target_pairs={{0,4},{1,5},{2,6},{3,7},{8,12},{9,13},{10,14},{11,15},{16,20},{17,... | collective-permute-start | bytes 77192 | tf_op jit(solution)/shard_map/ppermute | solution.py:17
  49.7 1.3 %collective-permute-start.9 = (f32[4,4,3,134]{3,0,2,1:T(4,128)S(1)}, f32[4,4,3,134]{3,0,2,1:T(4,128)S(1)}, u32[]{:S(2)}, u32[]{:S(2)}) collective-permute-start(f32[4,4,3,134]{3,0,2,1:T(4,128)S(1)} %get-tuple-element.32), channel_id=1, source_target_pairs={{4,0},{5,1},{6,2},{7,3},{12,8},{13,9},{14,10},{15,11},{20,16},{21,... | collective-permute-start | bytes 77192 | tf_op jit(solution)/shard_map/ppermute | solution.py:18
  51.4 4.3 %collective-permute-done.9 = f32[4,4,3,134]{3,0,2,1:T(4,128)S(1)} collective-permute-done((f32[4,4,3,134]{3,0,2,1:T(4,128)S(1)}, f32[4,4,3,134]{3,0,2,1:T(4,128)S(1)}, u32[]{:S(2)}, u32[]{:S(2)}) %collective-permute-start.9) | collective-permute-done | bytes 25760 | tf_op jit(solution)/shard_map/ppermute | solution.py:18
  56.2 3.2 %collective-permute-start.10 = (f32[4,3,22,134]{3,0,2,1:T(4,128)S(1)}, f32[4,3,22,134]{3,0,2,1:T(4,128)S(1)}, u32[]{:S(2)}, u32[]{:S(2)}) collective-permute-start(f32[4,3,22,134]{3,0,2,1:T(4,128)S(1)} %get-tuple-element.33), channel_id=1, source_target_pairs={{0,1},{1,2},{2,3},{4,5},{5,6},{6,7},{8,9},{9,10},{10,11},{12,13},{... | collective-permute-start | bytes 424520 | tf_op jit(solution)/shard_map/ppermute | solution.py:17
  59.4 1.5 %collective-permute-start.11 = (f32[4,3,22,134]{3,0,2,1:T(4,128)S(1)}, f32[4,3,22,134]{3,0,2,1:T(4,128)S(1)}, u32[]{:S(2)}, u32[]{:S(2)}) collective-permute-start(f32[4,3,22,134]{3,0,2,1:T(4,128)S(1)} %get-tuple-element.34), channel_id=1, source_target_pairs={{1,0},{2,1},{3,2},{5,4},{6,5},{7,6},{9,8},{10,9},{11,10},{13,12},{... | collective-permute-start | bytes 424520 | tf_op jit(solution)/shard_map/ppermute | solution.py:18
  60.9 0.7 copy.54
  61.6 3.4 %collective-permute-done.11 = f32[4,3,22,134]{3,0,2,1:T(4,128)S(1)} collective-permute-done((f32[4,3,22,134]{3,0,2,1:T(4,128)S(1)}, f32[4,3,22,134]{3,0,2,1:T(4,128)S(1)}, u32[]{:S(2)}, u32[]{:S(2)}) %collective-permute-start.11) | collective-permute-done | bytes 141536 | tf_op jit(solution)/shard_map/ppermute | solution.py:18
  65.0 0.5 pad_maximum_fusion
  66.2 0.5 broadcast_multiply_fusion
  66.8 2.4 %broadcast_multiply_fusion.1 = (f32[3,8,20,132]{3,0,2,1:T(4,128)S(1)}, f32[3,8,20,132]{3,0,2,1:T(4,128)S(1)}) fusion(f32[8,20,132]{2,1,0:T(8,128)S(1)} %get-tuple-element.40, f32[3,10,22,134]{3,0,2,1:T(4,128)S(1)} %get-tuple-element.15, f32[8,20,132]{2,1,0:T(8,128)S(1)} %get-tuple-element.39, f32[4,10,22,134]{3,0,2,1:T(4,128)S(1)} %pad_maximum_fusion, ...), kind=kLoop, calls=%fused_computation.35 | loop fusion | flops 760320 | bytes 2703360 | tf_op jit(solution)/shard_map/mul | solution.py:57
  69.2 1.7 %broadcast_multiply_fusion.2 = (f32[3,6,18,130]{3,0,2,1:T(4,128)S(1)}, f32[3,6,18,130]{3,0,2,1:T(4,128)S(1)}) fusion(f32[6,18,130]{2,1,0:T(8,128)S(1)} %get-tuple-element.38, f32[3,8,20,132]{3,0,2,1:T(4,128)S(1)} %get-tuple-element.13, f32[6,18,130]{2,1,0:T(8,128)S(1)} %get-tuple-element.37, f32[4,10,22,134]{3,0,2,1:T(4,128)S(1)} %pad_maximum_fusion, ...), kind=kLoop, calls=%fused_computation.46 | loop fusion | flops 505440 | bytes 1797120 | tf_op jit(solution)/shard_map/mul | solution.py:57
  70.9 0.5 multiply_reduce_fusion
  71.4 0.6 copy.55
  72.6 43.2 %all-gather.1 = f32[32,3,512]{2,1,0:T(4,128)S(1)} all-gather(f32[1,3,512]{2,1,0:T(4,128)S(1)} %convolution_bitcast_fusion.1), channel_id=2, replica_groups=mesh['circ'=4,'normal'=2,'span'=4] {'circ','normal','span'}, dimensions={0}, use_global_device_ids=true | all-gather | bytes 202752 | tf_op jit(solution)/shard_map/all_gather | solution.py:105
  115.8 0.6 constant_dynamic-slice_fusion
  (52 shorter events, 7.8 us)
Async XLA Ops:
  0.6 38.7 %copy-start = (f32[3,5]{1,0:T(4,128)S(1)}, f32[3,5]{1,0:T(4,128)}, u32[]{:S(2)}) copy-start(f32[3,5]{1,0:T(4,128)} %param.14) | copy-start | bytes 184
  0.6 1.0 copy-start.4
  1.8 12.3 %collective-permute-start = (f32[8,4,16,1]{3,2,1,0:T(8,128)S(1)}, f32[8,4,16,1]{3,2,1,0:T(8,128)S(1)}, u32[]{:S(2)}, u32[]{:S(2)}) collective-permute-start(f32[8,4,16,1]{3,2,1,0:T(8,128)S(1)} %get-tuple-element.35), channel_id=1, source_target_pairs={{0,8},{8,16},{16,24},{24,0},{1,9},{9,17},{17,25},{25,1},{2,10},{10... | collective-permute-start | bytes 6152 | tf_op jit(solution)/shard_map/ppermute | solution.py:17
  4.9 13.4 %collective-permute-start.1 = (f32[8,4,16,1]{3,2,1,0:T(8,128)S(1)}, f32[8,4,16,1]{3,2,1,0:T(8,128)S(1)}, u32[]{:S(2)}, u32[]{:S(2)}) collective-permute-start(f32[8,4,16,1]{3,2,1,0:T(8,128)S(1)} %get-tuple-element.36), channel_id=1, source_target_pairs={{8,0},{16,8},{24,16},{0,24},{9,1},{17,9},{25,17},{1,25},{10,2},{18... | collective-permute-start | bytes 6152 | tf_op jit(solution)/shard_map/ppermute | solution.py:18
  7.0 16.3 %copy-start.6 = (f32[3,5,5]{2,0,1:T(4,128)S(1)}, f32[3,5,5]{2,0,1:T(4,128)}, u32[]{:S(2)}) copy-start(f32[3,5,5]{2,0,1:T(4,128)} %param.12) | copy-start | bytes 904
  18.5 5.0 %collective-permute-start.2 = (f32[8,4,1,130]{3,2,1,0:T(1,128)S(1)}, f32[8,4,1,130]{3,2,1,0:T(1,128)S(1)}, u32[]{:S(2)}, u32[]{:S(2)}) collective-permute-start(f32[8,4,1,130]{3,2,1,0:T(1,128)S(1)} %get-tuple-element.27), channel_id=1, source_target_pairs={{0,4},{1,5},{2,6},{3,7},{8,12},{9,13},{10,14},{11,15},{16,20},{17,... | collective-permute-start | bytes 49928 | tf_op jit(solution)/shard_map/ppermute | solution.py:17
  22.0 5.8 %collective-permute-start.3 = (f32[8,4,1,130]{3,2,1,0:T(1,128)S(1)}, f32[8,4,1,130]{3,2,1,0:T(1,128)S(1)}, u32[]{:S(2)}, u32[]{:S(2)}) collective-permute-start(f32[8,4,1,130]{3,2,1,0:T(1,128)S(1)} %get-tuple-element.28), channel_id=1, source_target_pairs={{4,0},{5,1},{6,2},{7,3},{12,8},{13,9},{14,10},{15,11},{20,16},{21,... | collective-permute-start | bytes 49928 | tf_op jit(solution)/shard_map/ppermute | solution.py:18
  23.3 7.3 %copy-start.7 = (f32[3,5,5]{2,0,1:T(4,128)S(1)}, f32[3,5,5]{2,0,1:T(4,128)}, u32[]{:S(2)}) copy-start(f32[3,5,5]{2,0,1:T(4,128)} %param.13) | copy-start | bytes 904
  28.0 2.6 %collective-permute-start.5 = (f32[8,1,18,130]{3,2,1,0:T(8,128)S(1)}, f32[8,1,18,130]{3,2,1,0:T(8,128)S(1)}, u32[]{:S(2)}, u32[]{:S(2)}) collective-permute-start(f32[8,1,18,130]{3,2,1,0:T(8,128)S(1)} %get-tuple-element.25), channel_id=1, source_target_pairs={{0,1},{1,2},{2,3},{4,5},{5,6},{6,7},{8,9},{9,10},{10,11},{12,13},{... | collective-permute-start | bytes 224648 | tf_op jit(solution)/shard_map/ppermute | solution.py:17
  29.3 5.1 %collective-permute-start.4 = (f32[8,1,18,130]{3,2,1,0:T(8,128)S(1)}, f32[8,1,18,130]{3,2,1,0:T(8,128)S(1)}, u32[]{:S(2)}, u32[]{:S(2)}) collective-permute-start(f32[8,1,18,130]{3,2,1,0:T(8,128)S(1)} %get-tuple-element.26), channel_id=1, source_target_pairs={{1,0},{2,1},{3,2},{5,4},{6,5},{7,6},{9,8},{10,9},{11,10},{13,12},{... | collective-permute-start | bytes 224648 | tf_op jit(solution)/shard_map/ppermute | solution.py:18
  34.5 0.9 copy-start.1
  37.8 0.9 copy-start.3
  39.4 0.8 copy-start.2
  40.3 7.0 %collective-permute-start.6 = (f32[4,4,16,3]{3,0,2,1:T(4,128)S(1)}, f32[4,4,16,3]{3,0,2,1:T(4,128)S(1)}, u32[]{:S(2)}, u32[]{:S(2)}) collective-permute-start(f32[4,4,16,3]{3,0,2,1:T(4,128)S(1)} %get-tuple-element.41), channel_id=1, source_target_pairs={{0,8},{8,16},{16,24},{24,0},{1,9},{9,17},{17,25},{25,1},{2,10},{10... | collective-permute-start | bytes 9224 | tf_op jit(solution)/shard_map/ppermute | solution.py:17
  41.5 6.4 %collective-permute-start.7 = (f32[4,4,16,3]{3,0,2,1:T(4,128)S(1)}, f32[4,4,16,3]{3,0,2,1:T(4,128)S(1)}, u32[]{:S(2)}, u32[]{:S(2)}) collective-permute-start(f32[4,4,16,3]{3,0,2,1:T(4,128)S(1)} %get-tuple-element.42), channel_id=1, source_target_pairs={{8,0},{16,8},{24,16},{0,24},{9,1},{17,9},{25,17},{1,25},{10,2},{18... | collective-permute-start | bytes 9224 | tf_op jit(solution)/shard_map/ppermute | solution.py:18
  48.1 3.4 %collective-permute-start.8 = (f32[4,4,3,134]{3,0,2,1:T(4,128)S(1)}, f32[4,4,3,134]{3,0,2,1:T(4,128)S(1)}, u32[]{:S(2)}, u32[]{:S(2)}) collective-permute-start(f32[4,4,3,134]{3,0,2,1:T(4,128)S(1)} %get-tuple-element.31), channel_id=1, source_target_pairs={{0,4},{1,5},{2,6},{3,7},{8,12},{9,13},{10,14},{11,15},{16,20},{17,... | collective-permute-start | bytes 77192 | tf_op jit(solution)/shard_map/ppermute | solution.py:17
  49.7 6.0 %collective-permute-start.9 = (f32[4,4,3,134]{3,0,2,1:T(4,128)S(1)}, f32[4,4,3,134]{3,0,2,1:T(4,128)S(1)}, u32[]{:S(2)}, u32[]{:S(2)}) collective-permute-start(f32[4,4,3,134]{3,0,2,1:T(4,128)S(1)} %get-tuple-element.32), channel_id=1, source_target_pairs={{4,0},{5,1},{6,2},{7,3},{12,8},{13,9},{14,10},{15,11},{20,16},{21,... | collective-permute-start | bytes 77192 | tf_op jit(solution)/shard_map/ppermute | solution.py:18
  56.2 5.4 %collective-permute-start.10 = (f32[4,3,22,134]{3,0,2,1:T(4,128)S(1)}, f32[4,3,22,134]{3,0,2,1:T(4,128)S(1)}, u32[]{:S(2)}, u32[]{:S(2)}) collective-permute-start(f32[4,3,22,134]{3,0,2,1:T(4,128)S(1)} %get-tuple-element.33), channel_id=1, source_target_pairs={{0,1},{1,2},{2,3},{4,5},{5,6},{6,7},{8,9},{9,10},{10,11},{12,13},{... | collective-permute-start | bytes 424520 | tf_op jit(solution)/shard_map/ppermute | solution.py:17
  59.4 5.6 %collective-permute-start.11 = (f32[4,3,22,134]{3,0,2,1:T(4,128)S(1)}, f32[4,3,22,134]{3,0,2,1:T(4,128)S(1)}, u32[]{:S(2)}, u32[]{:S(2)}) collective-permute-start(f32[4,3,22,134]{3,0,2,1:T(4,128)S(1)} %get-tuple-element.34), channel_id=1, source_target_pairs={{1,0},{2,1},{3,2},{5,4},{6,5},{7,6},{9,8},{10,9},{11,10},{13,12},{... | collective-permute-start | bytes 424520 | tf_op jit(solution)/shard_map/ppermute | solution.py:18
  69.2 1.7 %copy-start.5 = (f32[4,16,128]{2,1,0:T(8,128)S(1)}, f32[4,16,128]{2,1,0:T(8,128)}, u32[]{:S(2)}) copy-start(f32[4,16,128]{2,1,0:T(8,128)} %param.16) | copy-start | bytes 98308
  71.4 0.7 copy-start.8
